TPU v7x, 128 devices: a whole 4x4x4 slice. The times are simulated.
128 devices in a mesh: img: 8 (over y, core), fsdp: 16 (over x, z).
Axes of the slice: x: 4, y: 4, z: 4, core: 2. Of those that a mesh axis runs over, the one named last changes fastest.
Arguments:
- text_states: bfloat16 [4096, 8192], P('img', 'fsdp'), may hold values from -100 to 100, as said below
- text_gain: float32 [8192], P('fsdp'), may hold values from 0.1 to 1.9
- gate_scale: float32 [8192], P('fsdp'), may hold values from 0.3 to 1.5
- live_counts: int32 [8], P('img'), may hold values from 1 to 512, 3072 in all
- token_slot: int32 [8, 512], P('img'), may hold values from 0 to 7, never falling along the last dimension, each value on 1 to 256 neighbouring positions
- wanted_images: int32 [8, 8], replicated, may hold values from 0 to 31, as said below
- patches: bfloat16 [32, 256, 1280], P('img', None, 'fsdp'), may hold values from -100 to 100, as said below
- latent_init: bfloat16 [64, 1280], replicated, may hold values from -100 to 100, as said below
- context_gain: float32 [1280], replicated, may hold values from 0.1 to 1.9
- latent_gain: float32 [1280], replicated, may hold values from 0.1 to 1.9
- res_query: bfloat16 [1280, 1536], P(None, 'fsdp'), may hold values from -0.15625 to 0.15625
- res_key: bfloat16 [1280, 1536], P(None, 'fsdp'), may hold values from -0.15625 to 0.15625
- res_value: bfloat16 [1280, 1536], P(None, 'fsdp'), may hold values from -0.15625 to 0.15625
- res_out: bfloat16 [1536, 1280], P('fsdp'), may hold values from -0.21875 to 0.21875
- final_gain: float32 [1280], P('fsdp'), may hold values from 0.1 to 1.9
- cross_query: bfloat16 [8192, 8192], P('fsdp'), may hold values from -0.09375 to 0.09375
- cross_key: bfloat16 [1280, 8192], P('fsdp'), may hold values from -0.25 to 0.25
- cross_value: bfloat16 [1280, 8192], P('fsdp'), may hold values from -0.25 to 0.25
- cross_out: bfloat16 [8192, 8192], P('fsdp'), may hold values from -0.09375 to 0.09375
Outputs:
- layer_output: float32 [4096, 8192], P('img', 'fsdp')
Inputs may be any that keep to these rules, and one draw needn't show every extreme that they name: `wanted_images`: image i is held by owner i // 4 along img. A row lists 8 distinct images; every owner that appears in a row has exactly 2 of its images there. `token_slot`: along a shard's tokens the slot never falls, and every slot of the shard is used. Tokens of shard s at positions live_counts[s] and beyond are padding. `text_states`: real values. `patches`: real values. `latent_init`: real values.
All inputs are finite; a program needn't handle non-finite values.
Results may differ from a plain program's by a relative error of at most 0.0075.
Values may be sent and summed in bfloat16 or wider, within the bound.
No kernel may reach another device: no remote copies, remote signals or barrier semaphores. Data moves between devices by JAX's collectives and lax.ppermute only.
A program may use at most 128 MiB of HBM per device.

v0:
```python
import jax
import jax.numpy as jnp
from jax import lax
from jax.sharding import PartitionSpec as P

D = 8192
HEAD = 128
RHD = 96
PAIR = 2
eps_norm = 1e-05
eps_rms = 1e-06


def layer_norm(values, gain_vec):
    values = values.astype(jnp.float32)
    row_mean = jnp.mean(values, -1, keepdims=True)
    spread = jnp.mean(values * values, -1, keepdims=True) - row_mean * row_mean
    return (values - row_mean) * lax.rsqrt(spread + eps_norm) * gain_vec


def route_tables(wanted_images, per_owner, pair_slots):
    owners = wanted_images // per_owner
    slot_total = wanted_images.shape[1]
    positions = jnp.arange(slot_total, dtype=jnp.int32)
    before = (owners[:, :, None] == owners[:, None, :]) & (
        positions[None, None, :] < positions[None, :, None]
    )
    slot_rank = jnp.sum(before.astype(jnp.int32), axis=2)
    rank_hot = (
        slot_rank[:, :, None] == jnp.arange(pair_slots, dtype=jnp.int32)[None, None, :]
    ).astype(jnp.float32)
    return (owners, rank_hot)


def pack_rows(row_data, wanted_images, my_shard, per_owner, pair_slots):
    owners, rank_hot = route_tables(wanted_images, per_owner, pair_slots)
    is_mine = (owners == my_shard).astype(jnp.float32)
    local_hot = (
        (wanted_images % per_owner)[:, :, None]
        == jnp.arange(per_owner, dtype=jnp.int32)[None, None, :]
    ).astype(jnp.float32)
    picker = jnp.einsum("scp,sci->spi", rank_hot * is_mine[:, :, None], local_hot).astype(
        jnp.bfloat16
    )
    return jnp.einsum("spi,if->spf", picker, row_data, preferred_element_type=jnp.float32).astype(
        jnp.bfloat16
    )


def unpack_rows(received, wanted_images, my_shard, per_owner, pair_slots):
    owners, rank_hot = route_tables(wanted_images, per_owner, pair_slots)
    owner_row = lax.dynamic_slice_in_dim(owners, my_shard, 1, 0)[0]
    rank_row = lax.dynamic_slice_in_dim(rank_hot, my_shard, 1, 0)[0]
    source_hot = (
        owner_row[:, None] == jnp.arange(received.shape[0], dtype=jnp.int32)[None, :]
    ).astype(jnp.float32)
    taker = (source_hot[:, :, None] * rank_row[:, None, :]).astype(jnp.bfloat16)
    return jnp.einsum("cop,opf->cf", taker, received, preferred_element_type=jnp.float32).astype(
        jnp.bfloat16
    )


def keyval_partial(flat_rows, cross_key, cross_value, head_cols, row_count):
    contract_first = (((0,), (1,)), ((), ()))
    block_count = row_count // (2 * head_cols)
    key_cols = lax.dot_general(
        cross_key, flat_rows, contract_first, preferred_element_type=jnp.float32
    )
    value_cols = lax.dot_general(
        cross_value, flat_rows, contract_first, preferred_element_type=jnp.float32
    )
    key_cols = key_cols.reshape(block_count, head_cols, flat_rows.shape[0])
    value_cols = value_cols.reshape(block_count, head_cols, flat_rows.shape[0])
    return jnp.concatenate([key_cols, value_cols], 1).reshape(row_count, flat_rows.shape[0])


def local(
    text_states,
    text_gain,
    gate_scale,
    live_counts,
    token_slot,
    wanted_images,
    patches,
    latent_init,
    context_gain,
    latent_gain,
    res_query,
    res_key,
    res_value,
    res_out,
    final_gain,
    cross_query,
    cross_key,
    cross_value,
    cross_out,
):
    my_feature = lax.axis_index("fsdp")
    my_shard = lax.axis_index("img")
    image_count = patches.shape[0]
    patch_count = patches.shape[1]
    feat_vis = patches.shape[2]
    latent_count = latent_init.shape[0]
    vis_width = latent_init.shape[1]
    res_cols = res_query.shape[1]
    res_heads = res_cols // RHD
    head_cols = cross_out.shape[0]
    token_count = text_states.shape[0]
    slot_count = wanted_images.shape[1]
    cross_heads = head_cols // HEAD
    contract_first = (((0,), (1,)), ((), ()))
    full_patches = lax.all_gather(patches, "fsdp", axis=2, tiled=True)
    context = layer_norm(full_patches, context_gain).astype(jnp.bfloat16)
    latent_normed = layer_norm(latent_init, latent_gain).astype(jnp.bfloat16)
    res_q_rows = jnp.dot(latent_normed, res_query, preferred_element_type=jnp.float32).astype(
        jnp.bfloat16
    )
    res_q_rows = res_q_rows.reshape(latent_count, res_heads, RHD)
    ctx_keys = jnp.einsum(
        "npv,vk->npk", context, res_key, preferred_element_type=jnp.float32
    ).astype(jnp.bfloat16)
    ctx_values = jnp.einsum(
        "npv,vk->npk", context, res_value, preferred_element_type=jnp.float32
    ).astype(jnp.bfloat16)
    lat_keys = jnp.dot(latent_normed, res_key, preferred_element_type=jnp.float32).astype(
        jnp.bfloat16
    )
    lat_values = jnp.dot(latent_normed, res_value, preferred_element_type=jnp.float32).astype(
        jnp.bfloat16
    )
    joined_shape = (image_count, latent_count, res_cols)
    key_rows = jnp.concatenate([ctx_keys, jnp.broadcast_to(lat_keys[None], joined_shape)], 1)
    value_rows = jnp.concatenate([ctx_values, jnp.broadcast_to(lat_values[None], joined_shape)], 1)
    key_rows = key_rows.reshape(image_count, patch_count + latent_count, res_heads, RHD)
    value_rows = value_rows.reshape(image_count, patch_count + latent_count, res_heads, RHD)
    res_scores = jnp.einsum(
        "rhe,nkhe->nhrk", res_q_rows, key_rows, preferred_element_type=jnp.float32
    ) * RHD ** (-0.5)
    res_weights = jnp.exp(res_scores)
    res_weights = (res_weights / jnp.sum(res_weights, -1, keepdims=True)).astype(jnp.bfloat16)
    res_mixed = jnp.einsum(
        "nhrk,nkhe->nrhe", res_weights, value_rows, preferred_element_type=jnp.float32
    )
    res_mixed = res_mixed.astype(jnp.bfloat16).reshape(image_count * latent_count, res_cols)
    columns = res_out
    mixed_sum = lax.psum_scatter(
        lax.dot_general(
            columns, res_mixed, contract_first, preferred_element_type=jnp.float32
        ).astype(jnp.bfloat16),
        "fsdp",
        scatter_dimension=0,
        tiled=True,
    ).astype(jnp.float32)
    init_cols = lax.dynamic_slice_in_dim(latent_init, my_feature * feat_vis, feat_vis, 1).astype(
        jnp.float32
    )
    latents = init_cols[None] + jnp.transpose(mixed_sum).reshape(
        image_count, latent_count, feat_vis
    )
    sum_first, sum_second = lax.psum((jnp.sum(latents, -1), jnp.sum(latents * latents, -1)), "fsdp")
    row_mean = sum_first / vis_width
    spread = sum_second / vis_width - row_mean * row_mean
    resampled = (
        (latents - row_mean[..., None]) * lax.rsqrt(spread + eps_norm)[..., None] * final_gain
    ).astype(jnp.bfloat16)
    text_f = text_states.astype(jnp.float32)
    squares = lax.psum(jnp.sum(text_f * text_f, -1), "fsdp")
    normed = (text_f * lax.rsqrt(squares / D + eps_rms)[:, None] * text_gain).astype(jnp.bfloat16)
    columns = cross_query
    query_cols = lax.psum_scatter(
        lax.dot_general(columns, normed, contract_first, preferred_element_type=jnp.float32).astype(
            jnp.bfloat16
        ),
        "fsdp",
        scatter_dimension=0,
        tiled=True,
    )
    per_image = resampled.reshape(image_count, latent_count * feat_vis)
    outgoing = pack_rows(per_image, wanted_images, my_shard, image_count, PAIR)
    incoming = lax.all_to_all(outgoing, "img", split_axis=0, concat_axis=0, tiled=True)
    slot_latents = unpack_rows(incoming, wanted_images, my_shard, image_count, PAIR).reshape(
        slot_count * latent_count, feat_vis
    )
    slot_kv = lax.psum_scatter(
        keyval_partial(
            slot_latents, cross_key, cross_value, head_cols, 2 * head_cols * lax.axis_size("fsdp")
        ).astype(jnp.bfloat16),
        "fsdp",
        scatter_dimension=0,
        tiled=True,
    )
    kv_slots = jnp.transpose(slot_kv.reshape(2 * head_cols, slot_count, latent_count), (1, 0, 2))
    query_heads = query_cols.reshape(cross_heads, HEAD, token_count)
    slot_keys = kv_slots[:, :head_cols].reshape(slot_count, cross_heads, HEAD, latent_count)
    slot_values = kv_slots[:, head_cols:].reshape(slot_count, cross_heads, HEAD, latent_count)
    scores = jnp.einsum(
        "het,cher->htcr", query_heads, slot_keys, preferred_element_type=jnp.float32
    ) * HEAD ** (-0.5)
    slot_hot = (token_slot[0][:, None] == jnp.arange(slot_count, dtype=jnp.int32)[None, :]).astype(
        jnp.float32
    )
    weights = jnp.exp(scores) * slot_hot[None, :, :, None]
    weights = (weights / jnp.sum(weights, axis=(2, 3), keepdims=True)).astype(jnp.bfloat16)
    attended = jnp.einsum(
        "htcr,cher->het", weights, slot_values, preferred_element_type=jnp.float32
    )
    attended = attended.astype(jnp.bfloat16).reshape(head_cols, token_count)
    columns = cross_out
    projected_cols = lax.psum_scatter(
        lax.dot_general(
            columns, attended, (((0,), (0,)), ((), ())), preferred_element_type=jnp.float32
        ).astype(jnp.bfloat16),
        "fsdp",
        scatter_dimension=0,
        tiled=True,
    ).astype(jnp.float32)
    projected = jnp.transpose(projected_cols)
    positions = jnp.arange(token_count, dtype=jnp.int32)
    live_mask = (positions < live_counts[0]).astype(jnp.float32)[:, None]
    return text_f + jnp.tanh(gate_scale) * projected * live_mask


def solution(mesh):
    placed = (
        P("img", "fsdp"),
        P("fsdp"),
        P("fsdp"),
        P("img"),
        P("img", None),
        P(),
        P("img", None, "fsdp"),
        P(),
        P(),
        P(),
        P(None, "fsdp"),
        P(None, "fsdp"),
        P(None, "fsdp"),
        P("fsdp", None),
        P("fsdp"),
        P("fsdp", None),
        P("fsdp", None),
        P("fsdp", None),
        P("fsdp", None),
    )
    return jax.shard_map(
        local, mesh=mesh, in_specs=placed, out_specs=P("img", "fsdp"), check_vma=False
    )
```

profile of v0, /device:TPU:0, one launch (start us, length us, event | category | flops | bytes accessed | tf_op | source)
XLA Modules:
  0.0 494.0 jit_solution(16812852713913608499)
XLA Ops:
  6.5 0.0 all-gather.2.cloned.1.call-start
  6.6 0.7 all-gather.2.cloned.1.call-update
  7.3 0.0 reduce-scatter.13.cloned.1.call-start
  7.3 1.1 convert_reduce_fusion.1
  8.4 1.3 convolution_convert_fusion.10
  9.7 0.1 copy.37
  9.8 1.3 convolution_convert_fusion.11
  11.2 0.1 copy.35
  11.3 46.9 %all-gather.2.cloned.1.call-done = bf16[4,256,1280]{1,2,0:T(8,128)(2,1)} async-done(((bf16[4,256,80]{1,2,0:T(8,128)(2,1)}), bf16[4,256,1280]{1,2,0:T(8,128)(2,1)}) %all-gather.2.cloned.1.call-update) | async-done | bytes 2621456 | tf_op jit(solution)/shard_map/all_gather | solution.py:112
  58.2 2.4 convert_reduce_fusion
  60.6 2.8 convolution_convert_fusion.6
  63.5 0.6 fusion.69
  64.2 2.8 convolution_convert_fusion.7
  67.0 0.3 convolution_convert_fusion.8
  67.3 0.3 fusion.8
  67.7 1.1 copy.49
  68.7 0.0 reduce-scatter.13.cloned.1.call-update
  68.8 0.0 reduce-scatter.9.cloned.1.call-start
  68.8 0.1 dynamic-slice_convert_fusion
  68.9 0.2 fusion.15
  69.1 72.8 %reduce-scatter.13.cloned.1.call-done = bf16[80,256]{1,0:T(8,128)(2,1)} async-done(((bf16[1280,256]{1,0:T(8,128)(2,1)}), bf16[80,256]{1,0:T(8,128)(2,1)}) %reduce-scatter.13.cloned.1.call-update) | async-done | bytes 40976
  141.9 0.9 copy.50
  142.7 0.2 fusion.42
  142.9 0.1 reduce_sum.105
  143.0 0.1 reduce_sum.107
  143.1 38.6 %all-reduce = (f32[512]{0:T(512)S(1)}, f32[4,64]{1,0:T(4,128)S(1)}, f32[4,64]{1,0:T(4,128)S(1)}) all-reduce(f32[512]{0:T(512)S(1)} %fusion.15, f32[4,64]{1,0:T(4,128)S(1)} %reduce_sum.107, f32[4,64]{1,0:T(4,128)S(1)} %reduce_sum.105), channel_id=1, replica_groups=mesh['img'=8,'fsdp'=16] {'fsdp'}, use_global_device_ids=true, to_apply=%region_13.14 | all-reduce | flops 1024 | bytes 8192 | tf_op jit(solution)/shard_map/psum | solution.py:167
  181.7 10.2 %fusion = bf16[8192,512]{0,1:T(8,128)(2,1)} fusion(bf16[512,8192]{1,0:T(8,128)(2,1)} %param.34, bf16[512,512]{1,0:T(8,128)(2,1)S(1)} %copy-done.2, f32[512]{0:T(512)S(1)} %copy-done.14, f32[512]{0:T(512)S(1)} %add_rsqrt_fusion.1), kind=kOutput, calls=%fused_computation.5 | convolution fusion | flops 4300210176 | bytes 17305600 | tf_op jit(solution)/shard_map/dot_general | solution.py:171
  191.9 0.1 add.87
  192.0 0.5 copy-done.9
  192.6 0.1 mul.200
  192.7 0.3 convert_reduce_fusion.2
  193.0 0.1 convolution_convert_fusion.12
  193.2 0.1 mul.196
  193.3 0.2 mul.197
  193.4 0.1 sub.61
  193.5 0.2 sub.62
  193.7 0.1 reshape.193
  193.9 0.2 convolution_convert_fusion.4
  194.0 0.8 copy.39
  194.9 4.3 all-to-all-start
  199.2 0.2 reduce-scatter.7.cloned.1.call-start
  199.4 0.1 fusion.56
  199.5 6.2 %all-to-all-done = bf16[8,2,5120]{2,1,0:T(2,128)(2,1)S(1)} async-done(((bf16[8,2,5120]{2,1,0:T(2,128)(2,1)}), bf16[8,2,5120]{2,1,0:T(2,128)(2,1)S(1)}, u32[]{:S(2)}, u32[]{:S(2)}) %all-to-all-start) | async-done | bytes 163872 | tf_op jit(solution)/shard_map/all_to_all | solution.py:180
  205.6 0.3 fusion.2
  205.9 0.2 reshape.194
  206.1 5.6 %convolution_convert_fusion.3 = bf16[512,8192]{1,0:T(8,128)(2,1)} fusion(bf16[512,80]{1,0:T(8,128)(2,1)S(1)} %reshape.194, bf16[80,8192]{1,0:T(8,128)(2,1)S(1)} %copy-done), kind=kOutput, calls=%fused_computation.4 | convolution fusion | flops 675282944 | bytes 9781248 | tf_op jit(solution)/shard_map/dot_general | solution.py:66
  211.7 11.6 %copy.53 = bf16[64,8,16,512]{3,2,1,0:T(8,128)(2,1)} copy(bf16[64,8,16,512]{3,1,2,0:T(8,128)(2,1)} %bitcast.115) | data formatting | bytes 16777216
  223.2 5.5 %convolution_convert_fusion.2 = bf16[512,8192]{1,0:T(8,128)(2,1)} fusion(bf16[512,80]{1,0:T(8,128)(2,1)S(1)} %reshape.194, bf16[80,8192]{1,0:T(8,128)(2,1)S(1)} %copy-done.3), kind=kOutput, calls=%fused_computation.3 | convolution fusion | flops 675282944 | bytes 9781248 | tf_op jit(solution)/shard_map/dot_general | solution.py:69
  228.8 11.4 %copy.54 = bf16[64,8,16,512]{3,2,1,0:T(8,128)(2,1)} copy(bf16[64,8,16,512]{3,1,2,0:T(8,128)(2,1)} %bitcast.114) | data formatting | bytes 16777216
  240.2 8.4 %pad_maximum_fusion = bf16[16,1024,512]{1,0,2:T(8,128)(2,1)S(1)} fusion(bf16[16,512,512]{1,0,2:T(8,128)(2,1)} %bitcast.117, bf16[16,512,512]{1,0,2:T(8,128)(2,1)} %bitcast.116), kind=kLoop, calls=%fused_computation | loop fusion | flops 33554432 | bytes 33554432 | tf_op jit(solution)/shard_map/concatenate | solution.py:74
  248.6 12.0 %copy.55 = bf16[64,8,16,1024]{3,1,2,0:T(8,128)(2,1)} copy(bf16[64,8,16,1024]{3,2,1,0:T(8,128)(2,1)S(1)} %bitcast.113) | data formatting | bytes 33554432
  260.6 0.0 reduce-scatter.11.cloned.1.call-start
  260.7 0.6 copy-done.7
  261.3 13.3 %reduce-scatter.9.cloned.1.call-done = bf16[512,512]{0,1:T(8,128)(2,1)} async-done(((bf16[8192,512]{0,1:T(8,128)(2,1)}), bf16[512,512]{0,1:T(8,128)(2,1)}) %reduce-scatter.9.cloned.1.call-update) | async-done | bytes 524304 | tf_op jit(solution)/shard_map/reduce_scatter | solution.py:170
  274.5 1.3 copy.48
  275.8 112.3 %reduce-scatter.7.cloned.1.call-done = bf16[1024,512]{0,1:T(8,128)(2,1)} async-done(((bf16[16384,512]{0,1:T(8,128)(2,1)}), bf16[1024,512]{0,1:T(8,128)(2,1)}) %reduce-scatter.7.cloned.1.call-update) | async-done | bytes 1048592 | tf_op jit(solution)/shard_map/reduce_scatter | solution.py:184
  388.1 1.3 slice_bitcast_fusion.1
  389.4 0.9 fusion.7
  390.3 1.0 fusion.11
  391.4 0.2 slice-done
  391.6 1.5 slice-done.1
  393.1 6.9 %fusion.1 = bf16[8192,512]{0,1:T(8,128)(2,1)} fusion(bf16[512,512]{1,0:T(8,128)(2,1)S(1)} %bitcast.122, bf16[512,8192]{1,0:T(8,128)(2,1)S(1)} %bitcast.119), kind=kOutput, calls=%fused_computation.6 | convolution fusion | flops 4299161600 | bytes 17301504 | tf_op jit(solution)/shard_map/dot_general | solution.py:210
  400.8 84.4 %reduce-scatter.11.cloned.1.call-done = bf16[512,512]{0,1:T(8,128)(2,1)} async-done(((bf16[8192,512]{0,1:T(8,128)(2,1)}), bf16[512,512]{0,1:T(8,128)(2,1)}) %reduce-scatter.11.cloned.1.call-update) | async-done | bytes 524304 | tf_op jit(solution)/shard_map/reduce_scatter | solution.py:209
  485.3 2.2 convert_add_fusion
  (51 shorter events, 0.3 us)
Async XLA Ops:
  6.5 199.6 %copy-start = (bf16[80,8192]{1,0:T(8,128)(2,1)S(1)}, bf16[80,8192]{1,0:T(8,128)(2,1)}, u32[]{:S(2)}) copy-start(bf16[80,8192]{1,0:T(8,128)(2,1)} %param.35) | copy-start | bytes 3932164
  6.5 56.9 %copy-start.5 = (bf16[64,1280]{1,0:T(8,128)(2,1)S(1)}, bf16[64,1280]{1,0:T(8,128)(2,1)}, u32[]{:S(2)}) copy-start(bf16[64,1280]{1,0:T(8,128)(2,1)} %param.26) | copy-start | bytes 491524
  6.5 56.9 %copy-start.12 = (f32[1280]{0:T(1024)S(1)}, f32[1280]{0:T(1024)}, u32[]{:S(2)}) copy-start(f32[1280]{0:T(1024)} %param.28) | copy-start | bytes 15364
  6.5 56.9 %copy-start.10 = (bf16[1280,96]{0,1:T(8,128)(2,1)S(1)}, bf16[1280,96]{0,1:T(8,128)(2,1)}, u32[]{:S(2)}) copy-start(bf16[1280,96]{0,1:T(8,128)(2,1)} %param.29) | copy-start | bytes 737284
  6.5 51.6 %all-gather.2.cloned.1.call-start = ((), (), s32[]{:S(2)}) async-start(), calls=%async_computation.5 | async-start | bytes 2785280 | tf_op jit(solution)/shard_map/all_gather | solution.py:112
  7.3 134.6 %reduce-scatter.13.cloned.1.call-start = ((), (), s32[]{:S(2)}) async-start(), calls=%async_computation.9 | async-start | bytes 696320
  9.8 54.3 %copy-start.11 = (bf16[1280,96]{0,1:T(8,128)(2,1)S(1)}, bf16[1280,96]{0,1:T(8,128)(2,1)}, u32[]{:S(2)}) copy-start(bf16[1280,96]{0,1:T(8,128)(2,1)} %param.31) | copy-start | bytes 737284
  9.8 54.3 %copy-start.13 = (f32[1280]{0:T(1024)S(1)}, f32[1280]{0:T(1024)}, u32[]{:S(2)}) copy-start(f32[1280]{0:T(1024)} %param.27) | copy-start | bytes 15364
  63.4 3.9 copy-start.4
  64.1 4.8 copy-start.2
  64.1 117.5 %copy-start.14 = (f32[512]{0:T(512)S(1)}, f32[512]{0:T(512)}, u32[]{:S(2)}) copy-start(f32[512]{0:T(512)} %param.20) | copy-start | bytes 6148
  68.8 205.8 %reduce-scatter.9.cloned.1.call-start = ((), (), s32[]{:S(2)}) async-start(), calls=%async_computation.7 | async-start | bytes 8912896 | tf_op jit(solution)/shard_map/reduce_scatter | solution.py:170
  191.9 0.7 copy-start.9
  191.9 0.7 copy-start.6
  194.9 10.7 %all-to-all-start = ((bf16[8,2,5120]{2,1,0:T(2,128)(2,1)}), bf16[8,2,5120]{2,1,0:T(2,128)(2,1)S(1)}, u32[]{:S(2)}, u32[]{:S(2)}) async-start(bf16[8,2,5120]{2,1,0:T(2,128)(2,1)} %copy.39), calls=%async_computation | async-start | bytes 327680 | tf_op jit(solution)/shard_map/all_to_all | solution.py:180
  199.2 188.9 %reduce-scatter.7.cloned.1.call-start = ((), (), s32[]{:S(2)}) async-start(), calls=%async_computation.6 | async-start | bytes 17825792 | tf_op jit(solution)/shard_map/reduce_scatter | solution.py:184
  211.7 11.6 %copy-start.3 = (bf16[80,8192]{1,0:T(8,128)(2,1)S(1)}, bf16[80,8192]{1,0:T(8,128)(2,1)}, u32[]{:S(2)}) copy-start(bf16[80,8192]{1,0:T(8,128)(2,1)} %param.36) | copy-start | bytes 3932164
  260.6 0.7 copy-start.7
  260.6 224.7 %reduce-scatter.11.cloned.1.call-start = ((), (), s32[]{:S(2)}) async-start(), calls=%async_computation.8 | async-start | bytes 8912896 | tf_op jit(solution)/shard_map/reduce_scatter | solution.py:209
  389.4 2.2 slice-start
  390.3 2.8 slice-start.1
  400.0 0.8 copy-start.8
  400.0 87.5 %copy-start.1 = (bf16[80,8192]{1,0:T(8,128)(2,1)S(1)}, bf16[80,8192]{1,0:T(8,128)(2,1)}, u32[]{:S(2)}) copy-start(bf16[80,8192]{1,0:T(8,128)(2,1)} %param.35) | copy-start | bytes 3932164
Sparse Core Ops, SparseCore 0:
  9.5 48.6 all-gather.1
  68.9 72.9 reduce-scatter.12
  192.1 82.4 reduce-scatter.8
  277.8 110.2 reduce-scatter.6
  400.2 85.0 reduce-scatter.10
where the time goes:
time: 495 us; the launch traced here: 494 us
  waiting for transfers between devices  337 us (68%)
  local copies, waits for them, and re-layouts  44.7 us (9%)
  matrix products  40.3 us (8%)
  blocking collectives  38.6 us (8%)
  other arithmetic  14.9 us (3%)
  between operations  14.3 us (3%)
    reduce_scatter x1, waiting for transfers between devices, local(): lax.psum_scatter(keyval_partial(slot_latents, cross_key, cross_value, hea...  112 us
    reduce_scatter x1, waiting for transfers between devices, local(): lax.psum_scatter(lax.dot_general(columns, attended, (((0,), (0,)), ((), (...  84.4 us
    unnamed x6, waiting for transfers between devices  73.5 us
    all_gather x1, waiting for transfers between devices, local(): full_patches = lax.all_gather(patches, 'fsdp', axis=2, tiled=True)  46.9 us
    unnamed x40, local copies, waits for them, and re-layouts  41.2 us
    psum x1, blocking collectives, local(): squares = lax.psum(jnp.sum(text_f * text_f, -1), 'fsdp')  38.6 us
    reduce_scatter x1, waiting for transfers between devices, local(): lax.psum_scatter(lax.dot_general(columns, normed, contract_first, preferr...  13.3 us
    dot_general x1, matrix products, local(): lax.dot_general(columns, normed, contract_first, preferred_element_type=j...  10.2 us
  transfers between devices with their start and end apart: 6, of which 6 were waited for; matrix products, arithmetic and copies ran while one was open for 13% of the time, Pallas kernels for 0%

commit v1 on v0

--- a/solution.py
+++ b/solution.py
@@ -9,6 +9,11 @@
 PAIR = 2
 eps_norm = 1e-05
 eps_rms = 1e-06
+
+
+def link_notes_now(local_values, along_axis):
+    x_next = jnp.sum(jax.lax.all_gather(local_values, along_axis), 0)
+    return x_next
 
 
 def layer_norm(values, gain_vec):
@@ -164,7 +169,7 @@
         (latents - row_mean[..., None]) * lax.rsqrt(spread + eps_norm)[..., None] * final_gain
     ).astype(jnp.bfloat16)
     text_f = text_states.astype(jnp.float32)
-    squares = lax.psum(jnp.sum(text_f * text_f, -1), "fsdp")
+    squares = link_notes_now(jnp.sum(text_f * text_f, -1), "fsdp")
     normed = (text_f * lax.rsqrt(squares / D + eps_rms)[:, None] * text_gain).astype(jnp.bfloat16)
     columns = cross_query
     query_cols = lax.psum_scatter(

time: 495 us -> 461 us (0.931)
  waiting for transfers between devices: 337 us -> 277 us
  blocking collectives: 38.6 us -> 63.2 us
    all_gather x1, waiting for transfers between devices: 46.9 us -> 20.7 us  [local(): full_patches = lax.all_gather(patches, 'fsdp', axis=2, tiled=True)]
    all_gather x0 -> x1, blocking collectives: none -> 24.8 us  [link_notes_now(): x_next = jnp.sum(jax.lax.all_gather(local_values, along_axis), 0)]
    reduce_scatter x1, waiting for transfers between devices: 13.3 us -> 0.01 us  [local(): lax.psum_scatter(lax.dot_general(columns, normed, contract_first, preferr...]
    unnamed x6, waiting for transfers between devices: 73.5 us -> 62.3 us
    reduce_scatter x1, waiting for transfers between devices: 112 us -> 104 us  [local(): lax.psum_scatter(keyval_partial(slot_latents, cross_key, cross_value, hea...]
  transfers between devices with their start and end apart: 6 -> 6, of which waited for: 6 -> 5; matrix products, arithmetic and copies ran while one was open for 13% -> 16% of each run, Pallas kernels for 0% -> 0%
where the time goes in v1:
time: 461 us; the launch traced here: 460 us
  waiting for transfers between devices  277 us (60%)
  blocking collectives  63.2 us (14%)
  local copies, waits for them, and re-layouts  44.2 us (10%)
  matrix products  40.3 us (9%)
  other arithmetic  16.1 us (3%)
  between operations  14.3 us (3%)
  starting transfers between devices  4.73 us (1%)
    reduce_scatter x1, waiting for transfers between devices, local(): lax.psum_scatter(keyval_partial(slot_latents, cross_key, cross_value, hea...  104 us
    reduce_scatter x1, waiting for transfers between devices, local(): lax.psum_scatter(lax.dot_general(columns, attended, (((0,), (0,)), ((), (...  84.6 us
    unnamed x6, waiting for transfers between devices  62.3 us
    unnamed x40, local copies, waits for them, and re-layouts  40.7 us
    psum x1, blocking collectives, local(): lax.psum((jnp.sum(latents, -1), jnp.sum(latents * latents, -1)), 'fsdp')  38.4 us
    all_gather x1, blocking collectives, link_notes_now(): x_next = jnp.sum(jax.lax.all_gather(local_values, along_axis), 0)  24.8 us
    all_gather x1, waiting for transfers between devices, local(): full_patches = lax.all_gather(patches, 'fsdp', axis=2, tiled=True)  20.7 us
    dot_general x1, matrix products, local(): lax.dot_general(columns, normed, contract_first, preferred_element_type=j...  10.2 us
  transfers between devices with their start and end apart: 6, of which 5 were waited for; matrix products, arithmetic and copies ran while one was open for 16% of the time, Pallas kernels for 0%

profile of v1, /device:TPU:0, one launch (start us, length us, event | category | flops | bytes accessed | tf_op | source)
XLA Modules:
  0.0 460.2 jit_solution(15139078959241947730)
XLA Ops:
  6.5 0.7 all-gather.4.cloned.1.call-update
  7.3 0.0 reduce-scatter.13.cloned.1.call-start
  7.3 1.1 convert_reduce_fusion.1
  8.4 1.4 convolution_convert_fusion.10
  9.8 0.1 copy.37
  9.9 1.3 convolution_convert_fusion.11
  11.2 0.1 copy.35
  11.3 1.3 fusion.15
  12.6 24.8 %all-gather.1 = f32[16,1,512]{2,1,0:T(1,128)S(1)} all-gather(f32[1,1,512]{2,1,0:T(1,128)S(1)} %bitcast.125), channel_id=2, replica_groups=mesh['img'=8,'fsdp'=16] {'fsdp'}, dimensions={0}, use_global_device_ids=true | all-gather | bytes 34816 | tf_op jit(solution)/shard_map/all_gather | solution.py:15
  37.5 20.7 %all-gather.4.cloned.1.call-done = bf16[4,256,1280]{1,2,0:T(8,128)(2,1)} async-done(((bf16[4,256,80]{1,2,0:T(8,128)(2,1)}), bf16[4,256,1280]{1,2,0:T(8,128)(2,1)}) %all-gather.4.cloned.1.call-update) | async-done | bytes 2621456 | tf_op jit(solution)/shard_map/all_gather | solution.py:117
  58.2 2.4 convert_reduce_fusion
  60.6 2.8 convolution_convert_fusion.6
  63.5 0.6 fusion.69
  64.2 2.8 convolution_convert_fusion.7
  67.0 0.3 convolution_convert_fusion.8
  67.4 0.3 fusion.8
  67.7 1.1 copy.49
  68.8 0.0 reduce-scatter.13.cloned.1.call-update
  68.8 0.0 reduce-scatter.9.cloned.1.call-start
  68.8 10.2 %fusion = bf16[8192,512]{0,1:T(8,128)(2,1)} fusion(bf16[512,8192]{1,0:T(8,128)(2,1)} %param.34, bf16[512,512]{1,0:T(8,128)(2,1)S(1)} %copy-done.2, f32[512]{0:T(512)S(1)} %copy-done.14, f32[512]{0:T(512)S(1)} %add_rsqrt_fusion.1), kind=kOutput, calls=%fused_computation.5 | convolution fusion | flops 4300210176 | bytes 17305600 | tf_op jit(solution)/shard_map/dot_general | solution.py:176
  79.1 0.0 reduce-scatter.9.cloned.1.call-update
  79.1 0.1 dynamic-slice_convert_fusion
  79.2 0.1 add.89
  79.3 0.4 copy-done.9
  79.8 0.1 mul.200
  79.9 0.3 convert_reduce_fusion.2
  80.2 0.1 convolution_convert_fusion.12
  80.3 61.5 %reduce-scatter.13.cloned.1.call-done = bf16[80,256]{1,0:T(8,128)(2,1)} async-done(((bf16[1280,256]{1,0:T(8,128)(2,1)}), bf16[80,256]{1,0:T(8,128)(2,1)}) %reduce-scatter.13.cloned.1.call-update) | async-done | bytes 40976
  141.8 0.9 copy.50
  142.7 0.2 fusion.42
  142.9 0.1 reduce_sum.114
  143.0 0.1 reduce_sum.116
  143.1 38.4 %all-reduce = (f32[4,64]{1,0:T(4,128)S(1)}, f32[4,64]{1,0:T(4,128)S(1)}) all-reduce(f32[4,64]{1,0:T(4,128)S(1)} %reduce_sum.116, f32[4,64]{1,0:T(4,128)S(1)} %reduce_sum.114), channel_id=1, replica_groups=mesh['img'=8,'fsdp'=16] {'fsdp'}, use_global_device_ids=true, to_apply=%region_10.0 | all-reduce | flops 512 | bytes 4096 | tf_op jit(solution)/shard_map/psum | solution.py:165
  181.5 0.1 mul.196
  181.6 0.2 mul.197
  181.7 0.1 sub.61
  181.8 0.2 sub.62
  182.0 0.1 reshape.197
  182.2 0.2 convolution_convert_fusion.4
  182.3 0.8 copy.39
  183.2 4.4 all-to-all-start
  187.6 0.2 reduce-scatter.7.cloned.1.call-start
  187.8 0.1 fusion.56
  187.9 6.2 %all-to-all-done = bf16[8,2,5120]{2,1,0:T(2,128)(2,1)S(1)} async-done(((bf16[8,2,5120]{2,1,0:T(2,128)(2,1)}), bf16[8,2,5120]{2,1,0:T(2,128)(2,1)S(1)}, u32[]{:S(2)}, u32[]{:S(2)}) %all-to-all-start) | async-done | bytes 163872 | tf_op jit(solution)/shard_map/all_to_all | solution.py:185
  194.0 0.3 fusion.2
  194.3 0.2 reshape.198
  194.5 5.5 %convolution_convert_fusion.3 = bf16[512,8192]{1,0:T(8,128)(2,1)} fusion(bf16[512,80]{1,0:T(8,128)(2,1)S(1)} %reshape.198, bf16[80,8192]{1,0:T(8,128)(2,1)S(1)} %copy-done), kind=kOutput, calls=%fused_computation.4 | convolution fusion | flops 675282944 | bytes 9781248 | tf_op jit(solution)/shard_map/dot_general | solution.py:71
  200.0 11.3 %copy.53 = bf16[64,8,16,512]{3,2,1,0:T(8,128)(2,1)} copy(bf16[64,8,16,512]{3,1,2,0:T(8,128)(2,1)} %bitcast.116) | data formatting | bytes 16777216
  211.3 5.5 %convolution_convert_fusion.2 = bf16[512,8192]{1,0:T(8,128)(2,1)} fusion(bf16[512,80]{1,0:T(8,128)(2,1)S(1)} %reshape.198, bf16[80,8192]{1,0:T(8,128)(2,1)S(1)} %copy-done.3), kind=kOutput, calls=%fused_computation.3 | convolution fusion | flops 675282944 | bytes 9781248 | tf_op jit(solution)/shard_map/dot_general | solution.py:74
  216.9 11.2 %copy.54 = bf16[64,8,16,512]{3,2,1,0:T(8,128)(2,1)} copy(bf16[64,8,16,512]{3,1,2,0:T(8,128)(2,1)} %bitcast.115) | data formatting | bytes 16777216
  228.1 8.4 %pad_maximum_fusion = bf16[16,1024,512]{1,0,2:T(8,128)(2,1)S(1)} fusion(bf16[16,512,512]{1,0,2:T(8,128)(2,1)} %bitcast.118, bf16[16,512,512]{1,0,2:T(8,128)(2,1)} %bitcast.117), kind=kLoop, calls=%fused_computation | loop fusion | flops 33554432 | bytes 33554432 | tf_op jit(solution)/shard_map/concatenate | solution.py:79
  236.4 12.1 %copy.55 = bf16[64,8,16,1024]{3,1,2,0:T(8,128)(2,1)} copy(bf16[64,8,16,1024]{3,2,1,0:T(8,128)(2,1)S(1)} %bitcast.114) | data formatting | bytes 33554432
  248.5 0.0 reduce-scatter.11.cloned.1.call-start
  248.6 0.6 copy-done.7
  249.2 1.3 copy.48
  250.5 103.6 %reduce-scatter.7.cloned.1.call-done = bf16[1024,512]{0,1:T(8,128)(2,1)} async-done(((bf16[16384,512]{0,1:T(8,128)(2,1)}), bf16[1024,512]{0,1:T(8,128)(2,1)}) %reduce-scatter.7.cloned.1.call-update) | async-done | bytes 1048592 | tf_op jit(solution)/shard_map/reduce_scatter | solution.py:189
  354.1 1.3 slice_bitcast_fusion.1
  355.4 0.9 fusion.7
  356.3 1.0 fusion.11
  357.4 0.2 slice-done
  357.6 1.5 slice-done.1
  359.1 7.0 %fusion.1 = bf16[8192,512]{0,1:T(8,128)(2,1)} fusion(bf16[512,512]{1,0:T(8,128)(2,1)S(1)} %bitcast.123, bf16[512,8192]{1,0:T(8,128)(2,1)S(1)} %bitcast.120), kind=kOutput, calls=%fused_computation.6 | convolution fusion | flops 4299161600 | bytes 17301504 | tf_op jit(solution)/shard_map/dot_general | solution.py:215
  366.9 84.6 %reduce-scatter.11.cloned.1.call-done = bf16[512,512]{0,1:T(8,128)(2,1)} async-done(((bf16[8192,512]{0,1:T(8,128)(2,1)}), bf16[512,512]{0,1:T(8,128)(2,1)}) %reduce-scatter.11.cloned.1.call-update) | async-done | bytes 524304 | tf_op jit(solution)/shard_map/reduce_scatter | solution.py:214
  451.5 2.2 convert_add_fusion
  (53 shorter events, 0.3 us)
Async XLA Ops:
  6.5 188.0 %copy-start = (bf16[80,8192]{1,0:T(8,128)(2,1)S(1)}, bf16[80,8192]{1,0:T(8,128)(2,1)}, u32[]{:S(2)}) copy-start(bf16[80,8192]{1,0:T(8,128)(2,1)} %param.35) | copy-start | bytes 3932164
  6.5 51.7 %all-gather.4.cloned.1.call-start = ((), (), s32[]{:S(2)}) async-start(), calls=%async_computation.5 | async-start | bytes 2785280 | tf_op jit(solution)/shard_map/all_gather | solution.py:117
  7.3 134.6 %reduce-scatter.13.cloned.1.call-start = ((), (), s32[]{:S(2)}) async-start(), calls=%async_computation.9 | async-start | bytes 696320
  8.4 55.1 %copy-start.5 = (bf16[64,1280]{1,0:T(8,128)(2,1)S(1)}, bf16[64,1280]{1,0:T(8,128)(2,1)}, u32[]{:S(2)}) copy-start(bf16[64,1280]{1,0:T(8,128)(2,1)} %param.26) | copy-start | bytes 491524
  8.4 55.1 %copy-start.10 = (bf16[1280,96]{0,1:T(8,128)(2,1)S(1)}, bf16[1280,96]{0,1:T(8,128)(2,1)}, u32[]{:S(2)}) copy-start(bf16[1280,96]{0,1:T(8,128)(2,1)} %param.29) | copy-start | bytes 737284
  8.4 55.1 %copy-start.12 = (f32[1280]{0:T(1024)S(1)}, f32[1280]{0:T(1024)}, u32[]{:S(2)}) copy-start(f32[1280]{0:T(1024)} %param.28) | copy-start | bytes 15364
  11.3 52.8 %copy-start.11 = (bf16[1280,96]{0,1:T(8,128)(2,1)S(1)}, bf16[1280,96]{0,1:T(8,128)(2,1)}, u32[]{:S(2)}) copy-start(bf16[1280,96]{0,1:T(8,128)(2,1)} %param.31) | copy-start | bytes 737284
  11.3 52.8 %copy-start.13 = (f32[1280]{0:T(1024)S(1)}, f32[1280]{0:T(1024)}, u32[]{:S(2)}) copy-start(f32[1280]{0:T(1024)} %param.27) | copy-start | bytes 15364
  63.4 3.9 copy-start.4
  64.1 4.7 %copy-start.2 = (bf16[512,512]{1,0:T(8,128)(2,1)S(1)}, bf16[512,512]{1,0:T(8,128)(2,1)}, u32[]{:S(2)}) copy-start(bf16[512,512]{1,0:T(8,128)(2,1)} %param.19) | copy-start | bytes 1572868
  64.1 4.7 %copy-start.14 = (f32[512]{0:T(512)S(1)}, f32[512]{0:T(512)}, u32[]{:S(2)}) copy-start(f32[512]{0:T(512)} %param.20) | copy-start | bytes 6148
  68.8 180.4 %reduce-scatter.9.cloned.1.call-start = ((), (), s32[]{:S(2)}) async-start(), calls=%async_computation.7 | async-start | bytes 8912896 | tf_op jit(solution)/shard_map/reduce_scatter | solution.py:175
  79.1 0.7 copy-start.9
  79.1 0.7 copy-start.6
  183.2 10.8 %all-to-all-start = ((bf16[8,2,5120]{2,1,0:T(2,128)(2,1)}), bf16[8,2,5120]{2,1,0:T(2,128)(2,1)S(1)}, u32[]{:S(2)}, u32[]{:S(2)}) async-start(bf16[8,2,5120]{2,1,0:T(2,128)(2,1)} %copy.39), calls=%async_computation | async-start | bytes 327680 | tf_op jit(solution)/shard_map/all_to_all | solution.py:185
  187.6 166.5 %reduce-scatter.7.cloned.1.call-start = ((), (), s32[]{:S(2)}) async-start(), calls=%async_computation.6 | async-start | bytes 17825792 | tf_op jit(solution)/shard_map/reduce_scatter | solution.py:189
  200.0 11.3 %copy-start.3 = (bf16[80,8192]{1,0:T(8,128)(2,1)S(1)}, bf16[80,8192]{1,0:T(8,128)(2,1)}, u32[]{:S(2)}) copy-start(bf16[80,8192]{1,0:T(8,128)(2,1)} %param.36) | copy-start | bytes 3932164
  248.5 0.7 copy-start.7
  248.5 202.9 %reduce-scatter.11.cloned.1.call-start = ((), (), s32[]{:S(2)}) async-start(), calls=%async_computation.8 | async-start | bytes 8912896 | tf_op jit(solution)/shard_map/reduce_scatter | solution.py:214
  355.4 2.2 slice-start
  356.3 2.8 slice-start.1
  366.1 0.8 copy-start.8
  366.1 87.6 %copy-start.1 = (bf16[80,8192]{1,0:T(8,128)(2,1)S(1)}, bf16[80,8192]{1,0:T(8,128)(2,1)}, u32[]{:S(2)}) copy-start(bf16[80,8192]{1,0:T(8,128)(2,1)} %param.35) | copy-start | bytes 3932164
Sparse Core Ops, SparseCore 0:
  9.5 48.6 all-gather.3
  68.9 72.8 reduce-scatter.12
  145.3 85.2 reduce-scatter.8
  248.7 105.3 reduce-scatter.6
  366.2 85.1 reduce-scatter.10
